TPU v7x, 256 devices: a whole 4x4x8 slice. The times are simulated.
256 devices in a mesh: band: 16 (over x, y_hi, core), req: 16 (over y_lo, z).
Axes of the slice: x: 4, y: 4 (y_hi: 2, y_lo: 2; y = y_hi * 2 + y_lo), z: 8, core: 2. Of those that a mesh axis runs over, the one named last changes fastest.
Arguments:
- latents: bfloat16 [16, 64, 512, 320], P('req', 'band'), may hold values from -40 to 40
- request_time_embedding: bfloat16 [16, 1280], P('req'), may hold values from -6 to 6
- request_adapter: int32 [16, 1], P('req'), may hold values from 0 to 255, as said below
- adapter_stored_row: int32 [256], replicated, may hold values from 0 to 255, as said below
- first_conv_weight: bfloat16 [3, 3, 320, 320], replicated, may hold values from -0.109375 to 0.109375
- stored_down_weight: bfloat16 [256, 3, 3, 320, 64], P(('band', 'req')), may hold values from -0.109375 to 0.109375
- stored_up_weight: bfloat16 [256, 64, 320], P(('band', 'req')), may hold values from -0.75 to 0.75
- second_conv_weight: bfloat16 [3, 3, 320, 320], replicated, may hold values from -0.109375 to 0.109375
- time_projection_weight: bfloat16 [1280, 320], replicated, may hold values from -0.15625 to 0.15625
Outputs:
- block_out: bfloat16 [16, 64, 512, 320], P('req', 'band')
Inputs may be any that keep to these rules, and one draw needn't show every extreme that they name: `request_adapter`: ids of adapters. `adapter_stored_row`: each stored row appears once.
All inputs are finite; a program needn't handle non-finite values.
Results may differ from a plain program's by a relative error of at most 0.0038.
Values may be sent and summed in bfloat16 or wider, within the bound.
No kernel may reach another device: no remote copies, remote signals or barrier semaphores. Data moves between devices by JAX's collectives and lax.ppermute only.
A program may use at most 128 MiB of HBM per device.

v0:
```python
import jax
import jax.numpy as jnp
from jax import lax
from jax.sharding import PartitionSpec as P

G = 32


def with_halo(x, sides, width):
    for axis, dim in sides:
        count, length = (lax.axis_size(axis), x.shape[dim])
        up = [(i, (i + 1) % count) for i in range(count - 1)]
        down = [(j, i) for i, j in up]
        last = lax.slice_in_dim(x, length - width, length, axis=dim)
        initial = lax.slice_in_dim(x, 0, width, axis=dim)
        before = lax.ppermute(last, axis, up)
        after = lax.ppermute(initial, axis, down)
        x = jnp.concatenate([before, x, after], axis=dim)
    return x


def group_norm(field, groups, total_rows):
    requests, rows, width, channels = field.shape
    grouped = field.reshape(requests, rows, width, groups, channels // groups)
    count = total_rows * width * (channels // groups)
    sums = lax.psum(jnp.sum(grouped, axis=(1, 2, 4)), "band")
    center = (sums / count)[:, None, None, :, None]
    deviation = grouped - center
    spread = lax.psum(jnp.sum(deviation * deviation, axis=(1, 2, 4)), "band") / count
    normed = deviation * lax.rsqrt(spread + 1e-05)[:, None, None, :, None]
    return normed.reshape(field.shape)


def padded_field(field):
    extended = with_halo(field, (("band", 1),), 1)
    return jnp.pad(extended, ((0, 0), (0, 0), (1, 1), (0, 0)))


def convolve(padded, kernel, rows, width):
    total = None
    for row_tap in range(3):
        for col_tap in range(3):
            term = jnp.einsum(
                "qhwc,cd->qhwd",
                padded[:, row_tap : row_tap + rows, col_tap : col_tap + width],
                kernel[row_tap, col_tap],
                preferred_element_type=jnp.float32,
            )
            total = term if total is None else total + term
    return total


def convolve_each(padded, kernels, rows, width):
    total = None
    for row_tap in range(3):
        for col_tap in range(3):
            term = jnp.einsum(
                "qhwc,qcd->qhwd",
                padded[:, row_tap : row_tap + rows, col_tap : col_tap + width],
                kernels[:, row_tap, col_tap],
                preferred_element_type=jnp.float32,
            )
            total = term if total is None else total + term
    return total


def select_rows(slots, to_global, pieces):
    down_piece, up_piece = pieces
    count = down_piece.shape[0]
    stored = to_global(jnp.arange(count, dtype=jnp.int32))
    matches = stored[None, :] == slots[:, None]
    zero = jnp.zeros((), down_piece.dtype)
    down_pick = jnp.sum(
        jnp.where(matches[:, :, None, None, None, None], down_piece[None], zero), axis=1
    )
    up_pick = jnp.sum(jnp.where(matches[:, :, None, None], up_piece[None], zero), axis=1)
    return (down_pick, up_pick)


def slots_of(adapter_ids, adapter_stored_row):
    adapter_count = adapter_stored_row.shape[0]
    picked = adapter_ids == jnp.arange(adapter_count, dtype=jnp.int32)[None, :]
    return jnp.sum(jnp.where(picked, adapter_stored_row[None, :], 0), axis=1)


def shards(
    latents,
    request_time_embedding,
    request_adapter,
    adapter_stored_row,
    first_conv_weight,
    stored_down_weight,
    stored_up_weight,
    second_conv_weight,
    time_projection_weight,
):
    requests, rows, width, channels = latents.shape
    total_rows = rows * lax.axis_size("band")
    held_adapters = stored_down_weight.shape[0]
    req_count = lax.axis_size("req")
    slots = slots_of(request_adapter, adapter_stored_row)
    band_base = lax.axis_index("band") * (req_count * held_adapters)

    def column_global(gathered):
        return band_base + gathered

    part_down, part_up = select_rows(
        slots,
        column_global,
        (
            lax.all_gather(stored_down_weight, "req", axis=0, tiled=True),
            lax.all_gather(stored_up_weight, "req", axis=0, tiled=True),
        ),
    )
    sum_down, sum_up = (
        lax.psum(part_down, "band").astype(jnp.float32),
        lax.psum(part_up, "band").astype(jnp.float32),
    )
    chosen_down = sum_down.astype(jnp.bfloat16)
    chosen_up = sum_up.astype(jnp.bfloat16)
    shift = jnp.dot(
        jax.nn.silu(request_time_embedding.astype(jnp.float32)).astype(jnp.bfloat16),
        time_projection_weight,
        preferred_element_type=jnp.float32,
    )
    groups = G
    first = jax.nn.silu(group_norm(latents.astype(jnp.float32), groups, total_rows)).astype(
        jnp.bfloat16
    )
    first_padded = padded_field(first)
    main = convolve(first_padded, first_conv_weight, rows, width)
    lowrank = convolve_each(first_padded, chosen_down, rows, width).astype(jnp.bfloat16)
    lifted = jnp.einsum("qhwk,qkc->qhwc", lowrank, chosen_up, preferred_element_type=jnp.float32)
    hidden = main + lifted + shift[:, None, None, :]
    second = jax.nn.silu(group_norm(hidden, groups, total_rows)).astype(jnp.bfloat16)
    result = latents.astype(jnp.float32) + convolve(
        padded_field(second), second_conv_weight, rows, width
    )
    return result.astype(jnp.bfloat16)


def solution(mesh):
    in_specs = (
        P("req", "band", None, None),
        P("req", None),
        P("req", None),
        P(),
        P(),
        P(("band", "req"), None, None, None, None),
        P(("band", "req"), None, None),
        P(),
        P(),
    )
    out_specs = P("req", "band", None, None)
    return jax.shard_map(shards, mesh=mesh, in_specs=in_specs, out_specs=out_specs, check_vma=False)
```

profile of v0, /device:TPU:1, one launch (start us, length us, event | category | flops | bytes accessed | tf_op | source)
XLA Modules:
  0.0 536.1 jit_solution(17608430378172255338)
XLA Ops:
  6.5 0.7 all-gather.2.cloned.1.call-update
  7.3 1.6 convert_reduce_fusion
  9.1 93.4 %psum.42 = f32[1,32]{1,0:T(1,128)S(1)} all-reduce(f32[1,32]{1,0:T(1,128)S(1)} %bitcast.261), channel_id=1, replica_groups=mesh['band'=16,'req'=16] {'band'}, use_global_device_ids=true, to_apply=%region_2.3 | all-reduce | flops 32 | bytes 256 | tf_op jit(solution)/shard_map/psum | solution.py:26
  103.5 33.5 %psum.43 = f32[1,32]{1,0:T(1,128)S(1)} all-reduce(f32[1,32]{1,0:T(1,128)S(1)} %bitcast.262), channel_id=1, replica_groups=mesh['band'=16,'req'=16] {'band'}, use_global_device_ids=true, to_apply=%region_5.6 | all-reduce | flops 32 | bytes 256 | tf_op jit(solution)/shard_map/psum | solution.py:29
  137.2 1.0 fusion.8
  138.2 2.1 collective-permute-start
  140.3 4.1 collective-permute-start.1
  145.1 0.7 fusion.108
  145.7 0.6 add_compare_fusion
  146.7 28.0 %all_gather.7 = bf16[16,64,320]{2,1,0:T(8,128)(2,1)S(1)} all-gather(bf16[1,64,320]{2,1,0:T(8,128)(2,1)S(1)} %copy-done.13), channel_id=1, replica_groups=mesh['band'=16,'req'=16] {'req'}, dimensions={0}, use_global_device_ids=true | all-gather | bytes 696320 | tf_op jit(solution)/shard_map/all_gather | solution.py:112
  174.9 3.4 fusion.32
  178.3 64.7 %psum.45 = bf16[64,320]{1,0:T(8,128)(2,1)S(1)} all-reduce(bf16[64,320]{1,0:T(8,128)(2,1)S(1)} %select_reduce_fusion.1), channel_id=1, replica_groups=mesh['band'=16,'req'=16] {'band'}, use_global_device_ids=true, to_apply=%region_10.11 | all-reduce | flops 20480 | bytes 81920 | tf_op jit(solution)/shard_map/psum | solution.py:117
  243.0 3.4 fusion.56
  246.4 3.2 fusion.15
  249.7 2.5 fusion.54
  252.2 2.4 fusion.52
  254.6 2.5 fusion.51
  257.1 2.4 fusion.49
  259.4 2.5 fusion.47
  262.0 6.3 %select_reduce_fusion = bf16[3,3,320,64]{2,3,1,0:T(8,128)(2,1)} fusion(bf16[16,3,3,320,64]{3,4,2,1,0:T(8,128)(2,1)} %all-gather.2.cloned.1.call-done, pred[16]{0:T(512)(128)(4,1)S(1)} %add_compare_fusion), kind=kLoop, calls=%fused_computation.2 | loop fusion | flops 5713920 | bytes 6266896 | tf_op jit(solution)/shard_map/reduce_sum | solution.py:73
  268.3 3.8 fusion.60
  272.1 3.3 fusion.41
  275.4 132.5 %all-reduce.4.cloned.1.call-done = bf16[1,3,3,320,64]{3,4,2,1,0:T(8,128)(2,1)} async-done(((bf16[1,3,3,320,64]{3,4,2,1,0:T(8,128)(2,1)}), bf16[1,3,3,320,64]{3,4,2,1,0:T(8,128)(2,1)}) %all-reduce.4.cloned.1.call-update) | async-done | bytes 368656 | tf_op jit(solution)/shard_map/psum | solution.py:116
  407.9 1.8 fusion.34
  409.8 2.5 fusion.62
  413.4 0.6 fusion.48
  414.0 1.4 fusion.55
  415.4 1.2 fusion.46
  416.6 13.4 %fusion.118 = (f32[320]{0:T(512)S(1)}, f32[4,512,320]{1,2,0:T(8,128)}) fusion(f32[320]{0:T(512)S(1)} %convolution_reduce_fusion, bf16[64,320]{1,0:T(8,128)(2,1)S(1)} %psum.45, f32[4,512,64]{1,2,0:T(8,128)} %fusion.55, f32[4,512,64]{1,2,0:T(8,128)} %fusion.62, f32[4,512,64]{1,2,0:T(8,128)S(1)} %fusion.53, f32[4,512,64]{1,2,0:T(8,128)} %fusion.46, ...), kind=kOutput, calls=%fused_computation.158 | convolution fusion | flops 175636160 | bytes 29723904 | tf_op jit(solution)/shard_map/qhwk,qkc->qhwc/dot_general | solution.py:133
  430.2 33.8 %psum.46 = f32[1,32]{1,0:T(1,128)S(1)} all-reduce(f32[1,32]{1,0:T(1,128)S(1)} %bitcast.263), channel_id=1, replica_groups=mesh['band'=16,'req'=16] {'band'}, use_global_device_ids=true, to_apply=%region_13.14 | all-reduce | flops 32 | bytes 256 | tf_op jit(solution)/shard_map/psum | solution.py:26
  464.1 2.2 multiply_reduce_fusion
  466.5 36.5 %psum.47 = f32[1,32]{1,0:T(1,128)S(1)} all-reduce(f32[1,32]{1,0:T(1,128)S(1)} %bitcast.260), channel_id=1, replica_groups=mesh['band'=16,'req'=16] {'band'}, use_global_device_ids=true, to_apply=%region_16.17 | all-reduce | flops 32 | bytes 256 | tf_op jit(solution)/shard_map/psum | solution.py:29
  503.2 0.9 fusion.121
  504.2 1.9 collective-permute-start.2
  506.1 2.4 collective-permute-start.3
  508.6 2.8 fusion.68
  511.4 2.3 collective-permute-done.2
  513.6 2.4 collective-permute-done.3
  516.0 1.7 select_maximum_fusion
  517.7 0.9 fusion.21
  518.6 1.0 fusion.22
  519.6 0.9 fusion.23
  520.5 1.0 fusion.24
  521.6 0.9 fusion.29
  522.4 0.9 fusion.26
  523.3 0.9 fusion.18
  524.6 0.8 copy-done.9
  525.5 3.8 fusion.10
  (65 shorter events, 4.4 us)
Async XLA Ops:
  6.5 139.8 %copy-start = (bf16[1280,320]{0,1:T(8,128)(2,1)S(1)}, bf16[1280,320]{0,1:T(8,128)(2,1)}, u32[]{:S(2)}) copy-start(bf16[1280,320]{0,1:T(8,128)(2,1)} %param.17) | copy-start | bytes 2457604
  6.5 96.2 %copy-start.5 = (bf16[1,4,512,320]{2,3,1,0:T(8,128)(2,1)S(1)}, bf16[1,4,512,320]{2,3,1,0:T(8,128)(2,1)}, u32[]{:S(2)}) copy-start(bf16[1,4,512,320]{2,3,1,0:T(8,128)(2,1)} %param.9) | copy-start | bytes 3932164
  6.5 255.4 %all-gather.2.cloned.1.call-start = ((), (), s32[]{:S(2)}) async-start(), calls=%async_computation | async-start | bytes 7520256 | tf_op jit(solution)/shard_map/all_gather | solution.py:111
  7.3 400.7 %all-reduce.4.cloned.1.call-start = ((), (), s32[]{:S(2)}) async-start(), calls=%async_computation.1 | async-start | bytes 884736 | tf_op jit(solution)/shard_map/psum | solution.py:116
  102.7 42.3 %copy-start.15 = (s32[256]{0:T(256)S(1)}, s32[256]{0:T(256)}, u32[]{:S(2)}) copy-start(s32[256]{0:T(256)} %param.12) | copy-start | bytes 3076
  102.7 43.6 %copy-start.14 = (bf16[1,1280]{1,0:T(2,128)(2,1)S(1)}, bf16[1,1280]{1,0:T(2,128)(2,1)}, u32[]{:S(2)}) copy-start(bf16[1,1280]{1,0:T(2,128)(2,1)} %param.10) | copy-start | bytes 7684
  103.3 43.5 %copy-start.13 = (bf16[1,64,320]{2,1,0:T(8,128)(2,1)S(1)}, bf16[1,64,320]{2,1,0:T(8,128)(2,1)}, u32[]{:S(2)}) copy-start(bf16[1,64,320]{2,1,0:T(8,128)(2,1)} %param.15) | copy-start | bytes 122884
  138.1 104.9 %copy-start.2 = (bf16[1,4,512,320]{2,3,1,0:T(8,128)(2,1)}, bf16[1,4,512,320]{2,3,1,0:T(8,128)(2,1)S(1)}, u32[]{:S(2)}) copy-start(bf16[1,4,512,320]{2,3,1,0:T(8,128)(2,1)S(1)} %fusion.8) | copy-start | bytes 3932164
  138.2 104.8 %collective-permute-start = (bf16[1,1,512,320]{2,3,1,0:T(8,128)(2,1)S(1)}, bf16[1,1,512,320]{2,3,1,0:T(8,128)(2,1)S(1)}, u32[]{:S(2)}, u32[]{:S(2)}) collective-permute-start(bf16[1,1,512,320]{2,3,1,0:T(8,128)(2,1)S(1)} %get-tuple-element.7), channel_id=1, source_target_pairs={{0,16},{16,32},{32,48},{48,64},{64,80},{80,96},{96,112},{112,128},... | collective-permute-start | bytes 983048 | tf_op jit(solution)/shard_map/ppermute | solution.py:16
  140.3 106.1 %collective-permute-start.1 = (bf16[1,1,512,320]{2,3,1,0:T(8,128)(2,1)S(1)}, bf16[1,1,512,320]{2,3,1,0:T(8,128)(2,1)}, u32[]{:S(2)}, u32[]{:S(2)}) collective-permute-start(bf16[1,1,512,320]{2,3,1,0:T(8,128)(2,1)S(1)} %get-tuple-element.8), channel_id=1, source_target_pairs={{16,0},{32,16},{48,32},{64,48},{80,64},{96,80},{112,96},{128,112},... | collective-permute-start | bytes 983048 | tf_op jit(solution)/shard_map/ppermute | solution.py:17
  243.0 3.4 copy-start.7
  246.4 3.3 copy-start.10
  275.4 136.9 %copy-start.8 = (bf16[1,1,512,320]{2,3,1,0:T(8,128)(2,1)S(1)}, bf16[1,1,512,320]{2,3,1,0:T(8,128)(2,1)}, u32[]{:S(2)}) copy-start(bf16[1,1,512,320]{2,3,1,0:T(8,128)(2,1)} %copy-done.7) | copy-start | bytes 983044
  407.9 4.4 copy-start.3
  407.9 4.4 copy-start.12
  429.9 73.2 %copy-start.4 = (f32[4,512,320]{1,2,0:T(8,128)S(1)}, f32[4,512,320]{1,2,0:T(8,128)}, u32[]{:S(2)}) copy-start(f32[4,512,320]{1,2,0:T(8,128)} %get-tuple-element.10) | copy-start | bytes 7864324
  503.2 5.4 %copy-start.11 = (bf16[3,3,320,320]{3,2,1,0:T(8,128)(2,1)S(1)}, bf16[3,3,320,320]{3,2,1,0:T(8,128)(2,1)}, u32[]{:S(2)}) copy-start(bf16[3,3,320,320]{3,2,1,0:T(8,128)(2,1)} %param.16) | copy-start | bytes 5529604
  504.2 9.4 %collective-permute-start.2 = (bf16[1,1,512,320]{2,3,1,0:T(8,128)(2,1)S(1)}, bf16[1,1,512,320]{2,3,1,0:T(8,128)(2,1)S(1)}, u32[]{:S(2)}, u32[]{:S(2)}) collective-permute-start(bf16[1,1,512,320]{2,3,1,0:T(8,128)(2,1)S(1)} %get-tuple-element.5), channel_id=1, source_target_pairs={{0,16},{16,32},{32,48},{48,64},{64,80},{80,96},{96,112},{112,128},... | collective-permute-start | bytes 983048 | tf_op jit(solution)/shard_map/ppermute | solution.py:16
  506.1 9.9 %collective-permute-start.3 = (bf16[1,1,512,320]{2,3,1,0:T(8,128)(2,1)S(1)}, bf16[1,1,512,320]{2,3,1,0:T(8,128)(2,1)S(1)}, u32[]{:S(2)}, u32[]{:S(2)}) collective-permute-start(bf16[1,1,512,320]{2,3,1,0:T(8,128)(2,1)S(1)} %get-tuple-element.6), channel_id=1, source_target_pairs={{16,0},{32,16},{48,32},{64,48},{80,64},{96,80},{112,96},{128,112},... | collective-permute-start | bytes 983048 | tf_op jit(solution)/shard_map/ppermute | solution.py:17
  523.3 1.3 copy-start.6
  523.3 2.1 copy-start.9
  525.4 3.8 copy-start.1
Sparse Core Ops, SparseCore 0:
  9.1 91.5 all-gather.1
  268.4 139.4 all-reduce.3
where the time goes:
time: 537 us; the launch traced here: 536 us
  blocking collectives  290 us (54%)
  waiting for transfers between devices  138 us (26%)
  matrix products  61.5 us (11%)
  other arithmetic  19.3 us (4%)
  between operations  14.4 us (3%)
  starting transfers between devices  10.6 us (2%)
    psum x1, waiting for transfers between devices, shards(): lax.psum(part_down, 'band').astype(jnp.float32)  133 us
    psum x2, blocking collectives, group_norm(): sums = lax.psum(jnp.sum(grouped, axis=(1, 2, 4)), 'band')  127 us
    psum x2, blocking collectives, group_norm(): lax.psum(jnp.sum(deviation * deviation, axis=(1, 2, 4)), 'band') / count  70 us
    psum x1, blocking collectives, shards(): lax.psum(part_up, 'band').astype(jnp.float32)  64.7 us
    dot_general x18, matrix products, convolve(): jnp.einsum('qhwc,cd->qhwd', padded[:, row_tap:row_tap + rows, col_tap:col...  39.2 us
    all_gather x1, blocking collectives, shards(): lax.all_gather(stored_up_weight, 'req', axis=0, tiled=True)  28 us
    dot_general x1, matrix products, shards(): jnp.einsum('qhwk,qkc->qhwc', lowrank, chosen_up, preferred_element_type=j...  13.4 us
  transfers between devices with their start and end apart: 6, of which 3 were waited for; matrix products, arithmetic and copies ran while one was open for 7% of the time, Pallas kernels for 0%

commit v1 on v0

--- a/solution.py
+++ b/solution.py
@@ -109,7 +109,15 @@
         column_global,
         (
             lax.all_gather(stored_down_weight, "req", axis=0, tiled=True),
-            lax.all_gather(stored_up_weight, "req", axis=0, tiled=True),
+            jnp.concatenate(
+                lax.all_to_all(
+                    jnp.stack([stored_up_weight for _ in range(lax.psum(1, "req"))], axis=0),
+                    "req",
+                    0,
+                    0,
+                ),
+                axis=0,
+            ),
         ),
     )
     sum_down, sum_up = (

time: 537 us -> 452 us (0.84)
  waiting for transfers between devices: 138 us -> 73.5 us
  blocking collectives: 290 us -> 258 us
  starting transfers between devices: 10.6 us -> 21.2 us
    psum x1, waiting for transfers between devices: 133 us -> 68.3 us  [shards(): lax.psum(part_down, 'band').astype(jnp.float32)]
    all_gather x1 -> x0, blocking collectives: 28 us -> none  [shards(): lax.all_gather(stored_up_weight, 'req', axis=0, tiled=True)]
    all_to_all x0 -> x1, starting transfers between devices: none -> 10.2 us  [shards(): lax.all_to_all(jnp.stack([stored_up_weight for _ in range(lax.psum(1, 're...]
  transfers between devices with their start and end apart: 6 -> 7, of which waited for: 3 -> 3; matrix products, arithmetic and copies ran while one was open for 7% -> 10% of each run, Pallas kernels for 0% -> 0%
where the time goes in v1:
time: 452 us; the launch traced here: 451 us
  blocking collectives  258 us (57%)
  waiting for transfers between devices  73.5 us (16%)
  matrix products  59.4 us (13%)
  starting transfers between devices  21.2 us (5%)
  other arithmetic  18.9 us (4%)
  between operations  14.4 us (3%)
  local copies, waits for them, and re-layouts  5.07 us (1%)
    psum x2, blocking collectives, group_norm(): sums = lax.psum(jnp.sum(grouped, axis=(1, 2, 4)), 'band')  128 us
    psum x2, blocking collectives, group_norm(): lax.psum(jnp.sum(deviation * deviation, axis=(1, 2, 4)), 'band') / count  70.1 us
    psum x1, waiting for transfers between devices, shards(): lax.psum(part_down, 'band').astype(jnp.float32)  68.3 us
    psum x1, blocking collectives, shards(): lax.psum(part_up, 'band').astype(jnp.float32)  60.1 us
    dot_general x18, matrix products, convolve(): jnp.einsum('qhwc,cd->qhwd', padded[:, row_tap:row_tap + rows, col_tap:col...  37.3 us
    dot_general x1, matrix products, shards(): jnp.einsum('qhwk,qkc->qhwc', lowrank, chosen_up, preferred_element_type=j...  13.2 us
    all_to_all x1, starting transfers between devices, shards(): lax.all_to_all(jnp.stack([stored_up_weight for _ in range(lax.psum(1, 're...  10.2 us
  transfers between devices with their start and end apart: 7, of which 3 were waited for; matrix products, arithmetic and copies ran while one was open for 10% of the time, Pallas kernels for 0%

profile of v1, /device:TPU:1, one launch (start us, length us, event | category | flops | bytes accessed | tf_op | source)
XLA Modules:
  0.0 450.9 jit_solution(9425658248556156179)
XLA Ops:
  6.5 0.7 all-gather.2.cloned.1.call-update
  7.3 1.8 stack.2
  9.0 10.2 %all-to-all-start = ((bf16[16,1,64,320]{3,2,1,0:T(8,128)(2,1)}), bf16[16,1,64,320]{3,2,1,0:T(8,128)(2,1)}, u32[]{:S(2)}, u32[]{:S(2)}) async-start(bf16[16,1,64,320]{3,2,1,0:T(8,128)(2,1)} %stack.2), calls=%async_computation | async-start | bytes 1572864 | tf_op jit(solution)/shard_map/all_to_all | solution.py:113
  19.8 94.5 %psum.42 = f32[1,32]{1,0:T(1,128)S(1)} all-reduce(f32[1,32]{1,0:T(1,128)S(1)} %bitcast.267), channel_id=1, replica_groups=mesh['band'=16,'req'=16] {'band'}, use_global_device_ids=true, to_apply=%region_2.3 | all-reduce | flops 32 | bytes 256 | tf_op jit(solution)/shard_map/psum | solution.py:26
  115.2 33.6 %psum.43 = f32[1,32]{1,0:T(1,128)S(1)} all-reduce(f32[1,32]{1,0:T(1,128)S(1)} %bitcast.268), channel_id=1, replica_groups=mesh['band'=16,'req'=16] {'band'}, use_global_device_ids=true, to_apply=%region_5.6 | all-reduce | flops 32 | bytes 256 | tf_op jit(solution)/shard_map/psum | solution.py:29
  149.0 1.0 fusion.8
  150.0 2.2 collective-permute-start
  152.2 4.2 collective-permute-start.1
  157.1 0.7 fusion.109
  158.9 3.4 fusion.32
  162.3 0.7 copy-done.8
  163.0 2.9 fusion.15
  166.0 2.6 fusion.54
  168.5 2.3 fusion.52
  170.9 2.6 fusion.51
  173.4 2.3 fusion.49
  175.8 2.5 fusion.47
  178.3 2.4 fusion.41
  180.7 2.4 fusion.57
  183.0 6.3 %select_reduce_fusion = bf16[3,3,320,64]{2,3,1,0:T(8,128)(2,1)} fusion(bf16[16,3,3,320,64]{3,4,2,1,0:T(8,128)(2,1)} %all-gather.2.cloned.1.call-done, pred[16]{0:T(512)(128)(4,1)S(1)} %add_compare_fusion), kind=kLoop, calls=%fused_computation.2 | loop fusion | flops 5713920 | bytes 6266896 | tf_op jit(solution)/shard_map/reduce_sum | solution.py:73
  189.3 3.8 fusion.61
  193.2 1.3 fusion.56
  194.5 60.1 %psum.45 = bf16[64,320]{1,0:T(8,128)(2,1)S(1)} all-reduce(bf16[64,320]{1,0:T(8,128)(2,1)S(1)} %fusion.56), channel_id=1, replica_groups=mesh['band'=16,'req'=16] {'band'}, use_global_device_ids=true, to_apply=%region_10.11 | all-reduce | flops 20480 | bytes 81920 | tf_op jit(solution)/shard_map/psum | solution.py:125
  254.6 68.3 %all-reduce.4.cloned.1.call-done = bf16[1,3,3,320,64]{3,4,2,1,0:T(8,128)(2,1)} async-done(((bf16[1,3,3,320,64]{3,4,2,1,0:T(8,128)(2,1)}), bf16[1,3,3,320,64]{3,4,2,1,0:T(8,128)(2,1)}) %all-reduce.4.cloned.1.call-update) | async-done | bytes 368656 | tf_op jit(solution)/shard_map/psum | solution.py:124
  322.9 1.8 fusion.34
  324.8 2.5 fusion.63
  329.0 1.4 fusion.55
  330.4 1.2 fusion.46
  331.6 13.2 %fusion.119 = (f32[320]{0:T(512)S(1)}, f32[4,512,320]{1,2,0:T(8,128)}) fusion(f32[320]{0:T(512)S(1)} %convolution_reduce_fusion, bf16[64,320]{1,0:T(8,128)(2,1)S(1)} %psum.45, f32[4,512,64]{1,2,0:T(8,128)} %fusion.55, f32[4,512,64]{1,2,0:T(8,128)} %fusion.63, f32[4,512,64]{1,2,0:T(8,128)S(1)} %fusion.53, f32[4,512,64]{1,2,0:T(8,128)} %fusion.46, ...), kind=kOutput, calls=%fused_computation.159 | convolution fusion | flops 175636160 | bytes 29723904 | tf_op jit(solution)/shard_map/qhwk,qkc->qhwc/dot_general | solution.py:141
  345.0 33.8 %psum.46 = f32[1,32]{1,0:T(1,128)S(1)} all-reduce(f32[1,32]{1,0:T(1,128)S(1)} %bitcast.269), channel_id=1, replica_groups=mesh['band'=16,'req'=16] {'band'}, use_global_device_ids=true, to_apply=%region_13.14 | all-reduce | flops 32 | bytes 256 | tf_op jit(solution)/shard_map/psum | solution.py:26
  378.9 2.2 multiply_reduce_fusion
  381.3 36.5 %psum.47 = f32[1,32]{1,0:T(1,128)S(1)} all-reduce(f32[1,32]{1,0:T(1,128)S(1)} %bitcast.266), channel_id=1, replica_groups=mesh['band'=16,'req'=16] {'band'}, use_global_device_ids=true, to_apply=%region_16.17 | all-reduce | flops 32 | bytes 256 | tf_op jit(solution)/shard_map/psum | solution.py:29
  418.0 0.9 fusion.122
  419.0 1.9 collective-permute-start.2
  420.9 2.7 collective-permute-start.3
  423.6 2.8 fusion.69
  426.4 2.0 collective-permute-done.2
  428.4 2.4 collective-permute-done.3
  430.8 1.7 select_maximum_fusion
  432.5 0.9 fusion.21
  433.4 1.0 fusion.22
  434.4 0.9 fusion.23
  435.3 1.0 fusion.24
  436.4 0.9 fusion.29
  437.2 0.9 fusion.26
  438.1 0.9 fusion.18
  439.4 0.8 copy-done.10
  440.3 3.8 fusion.10
  (67 shorter events, 5.8 us)
Async XLA Ops:
  6.5 152.0 %copy-start = (bf16[1280,320]{0,1:T(8,128)(2,1)S(1)}, bf16[1280,320]{0,1:T(8,128)(2,1)}, u32[]{:S(2)}) copy-start(bf16[1280,320]{0,1:T(8,128)(2,1)} %param.17) | copy-start | bytes 2457604
  6.5 12.7 %copy-start.6 = (bf16[1,4,512,320]{2,3,1,0:T(8,128)(2,1)S(1)}, bf16[1,4,512,320]{2,3,1,0:T(8,128)(2,1)}, u32[]{:S(2)}) copy-start(bf16[1,4,512,320]{2,3,1,0:T(8,128)(2,1)} %param.9) | copy-start | bytes 3932164
  6.5 176.5 %all-gather.2.cloned.1.call-start = ((), (), s32[]{:S(2)}) async-start(), calls=%async_computation.1 | async-start | bytes 7520256 | tf_op jit(solution)/shard_map/all_gather | solution.py:111
  9.0 184.1 %all-to-all-start = ((bf16[16,1,64,320]{3,2,1,0:T(8,128)(2,1)}), bf16[16,1,64,320]{3,2,1,0:T(8,128)(2,1)}, u32[]{:S(2)}, u32[]{:S(2)}) async-start(bf16[16,1,64,320]{3,2,1,0:T(8,128)(2,1)} %stack.2), calls=%async_computation | async-start | bytes 1572864 | tf_op jit(solution)/shard_map/all_to_all | solution.py:113
  19.2 303.7 %all-reduce.4.cloned.1.call-start = ((), (), s32[]{:S(2)}) async-start(), calls=%async_computation.2 | async-start | bytes 884736 | tf_op jit(solution)/shard_map/psum | solution.py:124
  114.4 42.7 %copy-start.15 = (s32[256]{0:T(256)S(1)}, s32[256]{0:T(256)}, u32[]{:S(2)}) copy-start(s32[256]{0:T(256)} %param.12) | copy-start | bytes 3076
  114.4 44.1 %copy-start.14 = (bf16[1,1280]{1,0:T(2,128)(2,1)S(1)}, bf16[1,1280]{1,0:T(2,128)(2,1)}, u32[]{:S(2)}) copy-start(bf16[1,1280]{1,0:T(2,128)(2,1)} %param.10) | copy-start | bytes 7684
  149.9 12.3 %copy-start.2 = (bf16[1,4,512,320]{2,3,1,0:T(8,128)(2,1)}, bf16[1,4,512,320]{2,3,1,0:T(8,128)(2,1)S(1)}, u32[]{:S(2)}) copy-start(bf16[1,4,512,320]{2,3,1,0:T(8,128)(2,1)S(1)} %fusion.8) | copy-start | bytes 3932164
  150.0 12.3 %collective-permute-start = (bf16[1,1,512,320]{2,3,1,0:T(8,128)(2,1)S(1)}, bf16[1,1,512,320]{2,3,1,0:T(8,128)(2,1)S(1)}, u32[]{:S(2)}, u32[]{:S(2)}) collective-permute-start(bf16[1,1,512,320]{2,3,1,0:T(8,128)(2,1)S(1)} %get-tuple-element.7), channel_id=1, source_target_pairs={{0,16},{16,32},{32,48},{48,64},{64,80},{80,96},{96,112},{112,128},... | collective-permute-start | bytes 983048 | tf_op jit(solution)/shard_map/ppermute | solution.py:16
  152.2 10.8 %collective-permute-start.1 = (bf16[1,1,512,320]{2,3,1,0:T(8,128)(2,1)S(1)}, bf16[1,1,512,320]{2,3,1,0:T(8,128)(2,1)}, u32[]{:S(2)}, u32[]{:S(2)}) collective-permute-start(bf16[1,1,512,320]{2,3,1,0:T(8,128)(2,1)S(1)} %get-tuple-element.8), channel_id=1, source_target_pairs={{16,0},{32,16},{48,32},{64,48},{80,64},{96,80},{112,96},{128,112},... | collective-permute-start | bytes 983048 | tf_op jit(solution)/shard_map/ppermute | solution.py:17
  162.3 3.7 copy-start.11
  162.3 0.7 copy-start.8
  178.3 2.4 copy-start.3
  178.3 2.4 copy-start.9
  322.9 4.4 copy-start.4
  322.9 4.4 copy-start.13
  344.8 73.2 %copy-start.5 = (f32[4,512,320]{1,2,0:T(8,128)S(1)}, f32[4,512,320]{1,2,0:T(8,128)}, u32[]{:S(2)}) copy-start(f32[4,512,320]{1,2,0:T(8,128)} %get-tuple-element.10) | copy-start | bytes 7864324
  418.0 5.6 %copy-start.12 = (bf16[3,3,320,320]{3,2,1,0:T(8,128)(2,1)S(1)}, bf16[3,3,320,320]{3,2,1,0:T(8,128)(2,1)}, u32[]{:S(2)}) copy-start(bf16[3,3,320,320]{3,2,1,0:T(8,128)(2,1)} %param.16) | copy-start | bytes 5529604
  419.0 9.4 %collective-permute-start.2 = (bf16[1,1,512,320]{2,3,1,0:T(8,128)(2,1)S(1)}, bf16[1,1,512,320]{2,3,1,0:T(8,128)(2,1)S(1)}, u32[]{:S(2)}, u32[]{:S(2)}) collective-permute-start(bf16[1,1,512,320]{2,3,1,0:T(8,128)(2,1)S(1)} %get-tuple-element.5), channel_id=1, source_target_pairs={{0,16},{16,32},{32,48},{48,64},{64,80},{80,96},{96,112},{112,128},... | collective-permute-start | bytes 983048 | tf_op jit(solution)/shard_map/ppermute | solution.py:16
  420.9 9.9 %collective-permute-start.3 = (bf16[1,1,512,320]{2,3,1,0:T(8,128)(2,1)S(1)}, bf16[1,1,512,320]{2,3,1,0:T(8,128)(2,1)S(1)}, u32[]{:S(2)}, u32[]{:S(2)}) collective-permute-start(bf16[1,1,512,320]{2,3,1,0:T(8,128)(2,1)S(1)} %get-tuple-element.6), channel_id=1, source_target_pairs={{16,0},{32,16},{48,32},{64,48},{80,64},{96,80},{112,96},{128,112},... | collective-permute-start | bytes 983048 | tf_op jit(solution)/shard_map/ppermute | solution.py:17
  438.1 1.3 copy-start.7
  438.1 2.1 copy-start.10
  440.2 3.8 copy-start.1
Sparse Core Ops, SparseCore 0:
  9.1 103.7 all-gather.1
  189.5 133.4 all-reduce.3
